TPU v7x, 128 devices: a whole 4x4x4 slice. The times are simulated.
128 devices in a mesh: ctx: 16 (over z_lo, y, core), ch: 8 (over z_hi, x).
Axes of the slice: x: 4, y: 4, z: 4 (z_hi: 2, z_lo: 2; z = z_hi * 2 + z_lo), core: 2. Of those that a mesh axis runs over, the one named last changes fastest.
Arguments:
- inputs: bfloat16 [512, 512, 1024], P('ctx', None, 'ch'), may hold values from -600 to 600
- norm_gain: float32 [1024], P('ch'), may hold values from 0.1 to 1.9
- conv_taps: float32 [2, 3, 1024], P(None, None, 'ch'), may hold values from -3 to 3
- factor_one: bfloat16 [512, 512], replicated, may hold values from -0.25 to 0.25
- factor_two: bfloat16 [512, 512], replicated, may hold values from -0.25 to 0.25
- kernel: bfloat16 [512, 512, 1024], P(None, 'ctx', 'ch'), may hold values from -5 to 5
- grad_out: bfloat16 [512, 512, 1024], P('ctx', None, 'ch'), may hold values from -5 to 5
Outputs:
- input_grad: bfloat16 [512, 512, 1024], P('ctx', None, 'ch')
- kernel_grad: bfloat16 [512, 512, 1024], P(None, 'ctx', 'ch')
- factor_one_grad: float32 [512, 512], replicated
- factor_two_grad: float32 [512, 512], replicated
- gain_grad: float32 [1024], P('ch')
- taps_grad: float32 [2, 3, 1024], P(None, None, 'ch')
All inputs are finite; a program needn't handle non-finite values.
Results may differ from a plain program's by a relative error of at most 0.0081.
Values may be sent and summed in bfloat16 or wider, within the bound.
No kernel may reach another device: no remote copies, remote signals or barrier semaphores. Data moves between devices by JAX's collectives and lax.ppermute only.
A program may use at most 192 MiB of HBM per device.

v0:
```python
import math
import jax
import jax.numpy as jnp
from jax import lax
from jax.sharding import PartitionSpec as P

OUTER = 512
INNER = 512
WIDTH = 1024


def shifted(value, axis, steps):
    count = lax.axis_size(axis)
    initial, last = (max(0, -steps), min(count, count - steps))
    return lax.ppermute(value, axis, [(source, source + steps) for source in range(initial, last)])


def on_device(inputs, norm_gain, conv_taps, factor_one, factor_two, kernel, grad_out):
    local_outer, inner, chans = inputs.shape
    rows = local_outer * inner
    taps_count = conv_taps.shape[1]
    flat_in = inputs.reshape(rows, chans).astype(jnp.float32)
    squares = lax.psum(jnp.sum(flat_in * flat_in, axis=1), "ch")
    inverse = lax.rsqrt(squares / WIDTH + 1e-05)
    hat = flat_in * inverse[:, None]
    normed = (hat * norm_gain).astype(jnp.bfloat16)
    earlier = shifted(normed[rows - (taps_count - 1) :], "ctx", 1)
    extended = jnp.concatenate([earlier, normed], 0)
    value_pre = jnp.zeros((rows, chans), jnp.float32)
    gate_pre = jnp.zeros((rows, chans), jnp.float32)
    for offset in range(taps_count):
        window = extended[taps_count - 1 - offset : taps_count - 1 - offset + rows]
        value_pre = value_pre + conv_taps[0, offset] * window
        gate_pre = gate_pre + conv_taps[1, offset] * window
    mixed_in = value_pre.astype(jnp.bfloat16).reshape(local_outer, inner, chans)
    gate = jax.nn.sigmoid(gate_pre)
    cotangent = grad_out.reshape(rows, chans).astype(jnp.float32)
    section_one = jnp.einsum(
        "ijc,jk->ikc", mixed_in, factor_one, preferred_element_type=jnp.float32
    ).astype(jnp.bfloat16)
    out_grad = (cotangent * gate).astype(jnp.bfloat16).reshape(local_outer, inner, chans)
    columns = lax.all_to_all(section_one, "ctx", split_axis=1, concat_axis=0, tiled=True)
    kern = kernel.astype(jnp.float32)
    spectrum = (columns.astype(jnp.float32) * kern).astype(jnp.bfloat16)
    section_two = jnp.einsum(
        "ijc,ik->kjc", spectrum, factor_two, preferred_element_type=jnp.float32
    ).astype(jnp.bfloat16)
    back_rows = lax.all_to_all(section_two, "ctx", split_axis=0, concat_axis=1, tiled=True)
    grad_columns = lax.all_to_all(out_grad, "ctx", split_axis=1, concat_axis=0, tiled=True)
    grad_spec = jnp.einsum(
        "kjc,ik->ijc", grad_columns, factor_two, preferred_element_type=jnp.float32
    )
    kernel_grad = (grad_spec * columns.astype(jnp.float32)).astype(jnp.bfloat16)
    grad_section = (grad_spec * kern).astype(jnp.bfloat16)
    two_part = jnp.einsum("ijc,kjc->ik", spectrum, grad_columns, preferred_element_type=jnp.float32)
    grad_rows = lax.all_to_all(grad_section, "ctx", split_axis=0, concat_axis=1, tiled=True)
    back_flat = back_rows.reshape(rows, chans).astype(jnp.float32)
    grad_gate_pre = cotangent * back_flat * gate * (1.0 - gate)
    grad_mixed = jnp.einsum(
        "ikc,jk->ijc", grad_rows, factor_one, preferred_element_type=jnp.float32
    ).reshape(rows, chans)
    one_part = jnp.einsum("ijc,ikc->jk", mixed_in, grad_rows, preferred_element_type=jnp.float32)
    one_total, two_total = lax.psum((one_part, two_part), ("ctx", "ch"))
    later_value, later_gate = shifted(
        (grad_mixed[: taps_count - 1], grad_gate_pre[: taps_count - 1]), "ctx", -1
    )
    ext_value = jnp.concatenate([grad_mixed, later_value], 0)
    ext_gate = jnp.concatenate([grad_gate_pre, later_gate], 0)
    grad_normed = jnp.zeros((rows, chans), jnp.float32)
    value_taps = []
    gate_taps = []
    for offset in range(taps_count):
        grad_normed = grad_normed + conv_taps[0, offset] * ext_value[offset : offset + rows]
        grad_normed = grad_normed + conv_taps[1, offset] * ext_gate[offset : offset + rows]
        window = extended[taps_count - 1 - offset : taps_count - 1 - offset + rows]
        value_taps.append(jnp.sum(grad_mixed * window, axis=0))
        gate_taps.append(jnp.sum(grad_gate_pre * window, axis=0))
    tap_part = jnp.stack([jnp.stack(value_taps), jnp.stack(gate_taps)])
    gain_part = jnp.sum(grad_normed * hat, axis=0)
    gain_total, taps_total = lax.psum((gain_part, tap_part), "ctx")
    scaled = grad_normed * norm_gain
    row_mean = (
        lax.psum(jnp.sum(scaled * hat, axis=1).astype(jnp.bfloat16), "ch").astype(jnp.float32)
        / WIDTH
    )
    input_grad = (
        (inverse[:, None] * (scaled - hat * row_mean[:, None]))
        .astype(jnp.bfloat16)
        .reshape(local_outer, inner, chans)
    )
    seq_scale = 1.0 / math.sqrt(OUTER * INNER)
    factor_one_grad = one_total / math.sqrt(OUTER * WIDTH)
    factor_two_grad = two_total / math.sqrt(INNER * WIDTH)
    return (
        input_grad,
        kernel_grad,
        factor_one_grad,
        factor_two_grad,
        gain_total * seq_scale,
        taps_total * seq_scale,
    )


def solution(mesh):
    in_specs = (
        P("ctx", None, "ch"),
        P("ch"),
        P(None, None, "ch"),
        P(),
        P(),
        P(None, "ctx", "ch"),
        P("ctx", None, "ch"),
    )
    out_specs = (P("ctx", None, "ch"), P(None, "ctx", "ch"), P(), P(), P("ch"), P(None, None, "ch"))
    return jax.shard_map(
        on_device, mesh=mesh, in_specs=in_specs, out_specs=out_specs, check_vma=False
    )
```

profile of v0, /device:TPU:1, one launch (start us, length us, event | category | flops | bytes accessed | tf_op | source)
XLA Modules:
  0.0 595.7 jit_solution(9241242994487293887)
XLA Ops:
  17.5 7.1 %copy.44 = f32[32,512,128]{2,1,0:T(8,128)} copy(bf16[32,512,128]{1,2,0:T(8,128)(2,1)} %copy.43) | data formatting | bytes 12582912 | tf_op jit(solution)/shard_map/convert_element_type | solution.py:22
  24.6 75.1 %all-reduce.5.cloned.1.call-done = f32[16384]{0:T(1024)} async-done(((f32[16384]{0:T(1024)}), f32[16384]{0:T(1024)}) %all-reduce.5.cloned.1.call-update) | async-done | bytes 65552 | tf_op jit(solution)/shard_map/psum | solution.py:23
  106.2 9.4 %collective-permute-start = (bf16[2,128]{1,0:T(2,128)(2,1)S(1)}, bf16[2,128]{1,0:T(2,128)(2,1)S(1)}, u32[]{:S(2)}, u32[]{:S(2)}) collective-permute-start(bf16[2,128]{1,0:T(2,128)(2,1)S(1)} %slice.68), channel_id=1, source_target_pairs={{0,8},{8,16},{16,24},{24,32},{32,40},{40,48},{48,56},{56,64},{64,7... | collective-permute-start | bytes 1544 | tf_op jit(solution)/shard_map/ppermute | solution.py:15
  132.2 7.9 %copy.55 = bf16[32,512,128]{2,0,1:T(8,128)(2,1)} copy(bf16[32,512,128]{1,2,0:T(8,128)(2,1)} %convert_bitcast_fusion.3) | data formatting | bytes 8388608 | tf_op jit(solution)/shard_map/convert_element_type | solution.py:40
  152.6 48.9 %all-to-all-done.2 = bf16[32,512,128]{2,0,1:T(8,128)(2,1)} async-done(((bf16[32,512,128]{2,0,1:T(8,128)(2,1)}), bf16[32,512,128]{2,0,1:T(8,128)(2,1)}, u32[]{:S(2)}, u32[]{:S(2)}) %all-to-all-start.2) | async-done | bytes 4194336 | tf_op jit(solution)/shard_map/all_to_all | solution.py:42
  207.0 7.6 %copy.49 = bf16[512,32,128]{0,2,1:T(8,128)(2,1)} copy(bf16[512,32,128]{2,1,0:T(8,128)(2,1)} %param.12) | data formatting | bytes 8388608 | tf_op args[5]
  223.8 9.9 %copy.58 = f32[512,32,128]{0,2,1:T(8,128)} copy(f32[512,32,128]{2,1,0:T(8,128)} %bitcast.102) | data formatting | bytes 16777216 | tf_op jit(solution)/shard_map/convert_element_type | solution.py:44
  233.7 8.9 %convert_bitcast_fusion.2 = bf16[512,32,128]{0,2,1:T(8,128)(2,1)} fusion(bf16[512,512]{1,0:T(8,128)(2,1)S(1)} %copy-done, f32[512,32,128]{0,2,1:T(8,128)} %copy.58, bf16[512,32,128]{0,2,1:T(8,128)(2,1)} %copy.49), kind=kOutput, calls=%fused_computation.66 | convolution fusion | flops 2155872256 | bytes 17301504 | tf_op jit(solution)/shard_map/ijc,ik->kjc/dot_general | solution.py:45
  242.6 7.9 %copy.59 = bf16[512,32,128]{2,1,0:T(8,128)(2,1)} copy(bf16[512,32,128]{0,2,1:T(8,128)(2,1)} %convert_bitcast_fusion.2) | data formatting | bytes 8388608 | tf_op jit(solution)/shard_map/convert_element_type | solution.py:47
  250.6 11.9 %all-to-all-done = bf16[32,512,128]{2,0,1:T(8,128)(2,1)} async-done(((bf16[32,512,128]{2,0,1:T(8,128)(2,1)}), bf16[32,512,128]{2,0,1:T(8,128)(2,1)}, u32[]{:S(2)}, u32[]{:S(2)}) %all-to-all-start) | async-done | bytes 4194336 | tf_op jit(solution)/shard_map/all_to_all | solution.py:49
  271.7 12.6 %fusion.29 = (bf16[512,32,128]{0,2,1:T(8,128)(2,1)}, bf16[512,32,128]{0,2,1:T(8,128)(2,1)}) fusion(f32[512,32,128]{0,2,1:T(8,128)} %copy.58, bf16[512,32,128]{0,2,1:T(8,128)(2,1)S(1)} %copy-done.2, bf16[512,512]{1,0:T(8,128)(2,1)S(1)} %copy-done, bf16[512,32,128]{2,1,0:T(8,128)(2,1)S(1)} %bitcast.100), kind=kOutput, calls=%fused_computation.53 | convolution fusion | flops 2157969408 | bytes 25690112 | tf_op jit(solution)/shard_map/kjc,ik->ijc/dot_general | solution.py:50
  284.4 7.9 %copy.50 = bf16[512,32,128]{2,1,0:T(8,128)(2,1)} copy(bf16[512,32,128]{0,2,1:T(8,128)(2,1)} %get-tuple-element.42) | data formatting | bytes 8388608 | tf_op jit(solution)/shard_map/convert_element_type | solution.py:54
  292.3 31.2 %all-to-all-done.3 = bf16[512,32,128]{2,1,0:T(8,128)(2,1)} async-done(((bf16[512,32,128]{2,1,0:T(8,128)(2,1)}), bf16[512,32,128]{2,1,0:T(8,128)(2,1)}, u32[]{:S(2)}, u32[]{:S(2)}) %all-to-all-start.3) | async-done | bytes 4194336 | tf_op jit(solution)/shard_map/all_to_all | solution.py:48
  328.5 7.8 %copy.64 = bf16[512,32,128]{2,1,0:T(8,128)(2,1)} copy(bf16[512,32,128]{0,2,1:T(8,128)(2,1)} %get-tuple-element.41) | data formatting | bytes 8388608
  336.4 11.0 %fusion.35 = f32[512,512]{1,0:T(8,128)} fusion(bf16[512,32,128]{2,1,0:T(8,128)(2,1)} %bitcast.101, f32[512,32,128]{0,2,1:T(8,128)} %copy.58, bf16[512,32,128]{0,2,1:T(8,128)(2,1)} %copy.49), kind=kOutput, calls=%fused_computation.73 | convolution fusion | flops 2153775104 | bytes 17825792 | tf_op jit(solution)/shard_map/ijc,kjc->ik/dot_general | solution.py:55
  355.1 29.1 %all-to-all-done.1 = bf16[512,32,128]{2,1,0:T(8,128)(2,1)} async-done(((bf16[512,32,128]{2,1,0:T(8,128)(2,1)}), bf16[512,32,128]{2,1,0:T(8,128)(2,1)}, u32[]{:S(2)}, u32[]{:S(2)}) %all-to-all-start.1) | async-done | bytes 4194336 | tf_op jit(solution)/shard_map/all_to_all | solution.py:56
  393.1 10.3 %multiply_reduce_fusion = (f32[128]{0:T(128)S(1)}, f32[32,512,128]{1,2,0:T(8,128)}) fusion(f32[128]{0:T(128)S(1)} %copy-done.12, f32[32,512]{1,0:T(8,128)S(1)} %mul.250, bf16[32,512,128]{1,2,0:T(8,128)(2,1)} %copy.43, bf16[32,512,128]{2,1,0:T(8,128)(2,1)} %bitcast.108, bf16[512,512]{1,0:T(8,128)(2,1)S(1)} %copy-done.11), kind=kOutput, calls=%fused_computation.55 | convolution fusion | flops 2162163712 | bytes 17368064 | tf_op jit(solution)/shard_map/ikc,jk->ijc/dot_general | solution.py:59
  403.4 8.9 %copy.53 = f32[32,512,128]{2,1,0:T(8,128)} copy(f32[32,512,128]{1,2,0:T(8,128)} %get-tuple-element.50) | data formatting | bytes 16777216 | tf_op jit(solution)/shard_map/ikc,jk->ijc/transpose | solution.py:59
  413.0 14.0 %fusion.22 = (f32[128]{0:T(128)S(1)}, f32[128]{0:T(128)S(1)}, f32[128]{0:T(128)S(1)}, f32[128]{0:T(128)S(1)}, f32[128]{0:T(128)S(1)}, /*index=5*/f32[16384,128]{1,0:T(8,128)S(1)}) fusion(bf16[16384,128]{1,0:T(8,128)(2,1)} %copy-done.3, bf16[2,128]{1,0:T(2,128)(2,1)S(1)} %collective-permute-done, bf16[16384,128]{1,0:T(8,128)(2,1)} %copy-done.5, ...), kind=kLoop, calls=%fused_computation.41 | loop fusion | flops 60816768 | bytes 37753344 | tf_op jit(solution)/shard_map/reduce_sum | solution.py:77
  438.1 31.9 %multiply_reduce_fusion.1 = (f32[128]{0:T(128)S(1)}, bf16[16384]{0:T(1024)(128)(2,1)S(1)}, f32[16384,128]{1,0:T(8,128)}) fusion(f32[32,512,128]{2,1,0:T(8,128)} %copy.44, f32[16384]{0:T(1024)S(1)} %add_rsqrt_fusion, f32[128]{0:T(128)S(1)} %copy-done.12, f32[2,128]{1,0:T(2,128)S(1)} %collective-permute-done.2, f32[16384,128]{1,0:T(8,128)} %copy-done.6, ...), kind=kLoop, calls=%fused_computation.57 | loop fusion | flops 44023680 | bytes 33658880 | tf_op jit(solution)/shard_map/reduce_sum | solution.py:79
  470.1 31.7 %psum.43 = bf16[16384]{0:T(1024)(128)(2,1)S(1)} all-reduce(bf16[16384]{0:T(1024)(128)(2,1)S(1)} %get-tuple-element.25), channel_id=1, replica_groups=mesh['ctx'=16,'ch'=8] {'ch'}, use_global_device_ids=true, to_apply=%region_3.0 | all-reduce | flops 16384 | bytes 65536 | tf_op jit(solution)/shard_map/psum | solution.py:83
  501.8 11.5 %multiply_convert_fusion.1 = bf16[16384,128]{1,0:T(8,128)(2,1)} fusion(f32[16384,128]{1,0:T(8,128)} %get-tuple-element.38, f32[32,512,128]{2,1,0:T(8,128)} %copy.44, f32[16384]{0:T(1024)S(1)} %convert_multiply_fusion.15, f32[128]{0:T(128)S(1)} %copy-done.12, f32[16384]{0:T(1024)S(1)} %add_rsqrt_fusion), kind=kLoop, calls=%fused_computation.58 | loop fusion | flops 12582912 | bytes 21103104 | tf_op jit(solution)/shard_map/convert_element_type | solution.py:88
  513.3 31.7 %all-reduce.1 = (f32[128]{0:T(128)S(1)}, f32[2,3,128]{2,1,0:T(4,128)S(1)}) all-reduce(f32[128]{0:T(128)S(1)} %get-tuple-element.24, f32[2,3,128]{2,1,0:T(4,128)S(1)} %pad_maximum_fusion.3), channel_id=1, replica_groups=mesh['ctx'=16,'ch'=8] {'ctx'}, use_global_device_ids=true, to_apply=%region_7.0 | all-reduce | flops 896 | bytes 7168 | tf_op jit(solution)/shard_map/psum | solution.py:80
  546.2 39.4 %all-reduce.7.cloned.1.call-done = (f32[512,512]{1,0:T(8,128)}, f32[512,512]{1,0:T(8,128)}) async-done(((f32[512,512]{1,0:T(8,128)}, f32[512,512]{1,0:T(8,128)}), (f32[512,512]{1,0:T(8,128)}, f32[512,512]{1,0:T(8,128)})) %all-reduce.7.cloned.1.call-update) | async-done | bytes 2097168 | tf_op jit(solution)/shard_map/psum | solution.py:63
  (70 shorter events, 107.4 us)
Async XLA Ops:
  7.2 226.5 %copy-start = (bf16[512,512]{1,0:T(8,128)(2,1)S(1)}, bf16[512,512]{1,0:T(8,128)(2,1)}, u32[]{:S(2)}) copy-start(bf16[512,512]{1,0:T(8,128)(2,1)} %param.11) | copy-start | bytes 1572868
  7.2 92.5 %all-reduce.5.cloned.1.call-start = ((), (), s32[]{:S(2)}) async-start(), calls=%async_computation.4 | async-start | bytes 131072 | tf_op jit(solution)/shard_map/psum | solution.py:23
  13.7 87.0 %copy-start.12 = (f32[128]{0:T(128)S(1)}, f32[128]{0:T(128)}, u32[]{:S(2)}) copy-start(f32[128]{0:T(128)} %param.8) | copy-start | bytes 1540
  24.6 91.1 %copy-start.13 = (f32[2,3,128]{2,0,1:T(2,128)S(1)}, f32[2,3,128]{2,0,1:T(2,128)}, u32[]{:S(2)}) copy-start(f32[2,3,128]{2,0,1:T(2,128)} %param.9) | copy-start | bytes 9220
  99.7 16.6 %copy-start.9 = (bf16[32,512,128]{2,1,0:T(8,128)(2,1)S(1)}, bf16[32,512,128]{2,1,0:T(8,128)(2,1)}, u32[]{:S(2)}) copy-start(bf16[32,512,128]{2,1,0:T(8,128)(2,1)} %param.13) | copy-start | bytes 12582916
  106.2 16.6 %copy-start.3 = (bf16[16384,128]{1,0:T(8,128)(2,1)}, bf16[16384,128]{1,0:T(8,128)(2,1)S(1)}, u32[]{:S(2)}) copy-start(bf16[16384,128]{1,0:T(8,128)(2,1)S(1)} %multiply_convert_fusion.2) | copy-start | bytes 12582916
  106.2 10.1 %collective-permute-start = (bf16[2,128]{1,0:T(2,128)(2,1)S(1)}, bf16[2,128]{1,0:T(2,128)(2,1)S(1)}, u32[]{:S(2)}, u32[]{:S(2)}) collective-permute-start(bf16[2,128]{1,0:T(2,128)(2,1)S(1)} %slice.68), channel_id=1, source_target_pairs={{0,8},{8,16},{16,24},{24,32},{32,40},{40,48},{48,56},{56,64},{64,7... | collective-permute-start | bytes 1544 | tf_op jit(solution)/shard_map/ppermute | solution.py:15
  122.8 3.0 copy-start.5
  122.8 5.0 copy-start.11
  125.9 1.9 copy-start.7
  140.1 61.4 %all-to-all-start.2 = ((bf16[32,512,128]{2,0,1:T(8,128)(2,1)}), bf16[32,512,128]{2,0,1:T(8,128)(2,1)}, u32[]{:S(2)}, u32[]{:S(2)}) async-start(bf16[32,512,128]{2,0,1:T(8,128)(2,1)} %copy.55), calls=%async_computation.2 | async-start | bytes 8388608 | tf_op jit(solution)/shard_map/all_to_all | solution.py:42
  201.5 61.0 %all-to-all-start = ((bf16[32,512,128]{2,0,1:T(8,128)(2,1)}), bf16[32,512,128]{2,0,1:T(8,128)(2,1)}, u32[]{:S(2)}, u32[]{:S(2)}) async-start(bf16[32,512,128]{2,0,1:T(8,128)(2,1)} %copy.45), calls=%async_computation | async-start | bytes 8388608 | tf_op jit(solution)/shard_map/all_to_all | solution.py:49
  262.5 61.0 %all-to-all-start.3 = ((bf16[512,32,128]{2,1,0:T(8,128)(2,1)}), bf16[512,32,128]{2,1,0:T(8,128)(2,1)}, u32[]{:S(2)}, u32[]{:S(2)}) async-start(bf16[512,32,128]{2,1,0:T(8,128)(2,1)} %copy.59), calls=%async_computation.3 | async-start | bytes 8388608 | tf_op jit(solution)/shard_map/all_to_all | solution.py:48
  267.6 4.1 copy-start.2
  271.7 12.6 %copy-start.4 = (bf16[16,32,32,128]{3,2,1,0:T(8,128)(2,1)}, bf16[16,32,32,128]{3,2,1,0:T(8,128)(2,1)S(1)}, u32[]{:S(2)}) copy-start(bf16[16,32,32,128]{3,2,1,0:T(8,128)(2,1)S(1)} %copy.47) | copy-start | bytes 12582916
  323.4 60.7 %all-to-all-start.1 = ((bf16[512,32,128]{2,1,0:T(8,128)(2,1)}), bf16[512,32,128]{2,1,0:T(8,128)(2,1)}, u32[]{:S(2)}, u32[]{:S(2)}) async-start(bf16[512,32,128]{2,1,0:T(8,128)(2,1)} %copy.50), calls=%async_computation.1 | async-start | bytes 8388608 | tf_op jit(solution)/shard_map/all_to_all | solution.py:56
  328.5 257.0 %all-reduce.7.cloned.1.call-start = ((), (), s32[]{:S(2)}) async-start(), calls=%async_computation.5 | async-start | bytes 4194304 | tf_op jit(solution)/shard_map/psum | solution.py:63
  384.2 5.5 copy-start.8
  387.8 1.9 copy-start.10
  427.0 3.3 copy-start.6
  430.3 5.9 collective-permute-start.2
  432.9 5.3 collective-permute-start.1
  501.8 86.8 %copy-start.1 = (bf16[512,512]{1,0:T(8,128)(2,1)S(1)}, bf16[512,512]{1,0:T(8,128)(2,1)}, u32[]{:S(2)}) copy-start(bf16[512,512]{1,0:T(8,128)(2,1)} %param.11) | copy-start | bytes 1572868
Sparse Core Ops, SparseCore 0:
  17.6 82.0 all-reduce.4
  435.0 150.5 all-reduce.6
where the time goes:
time: 606 us; the launch traced here: 596 us
  waiting for transfers between devices  240 us (40%)
  local copies, waits for them, and re-layouts  108 us (18%)
  other arithmetic  84.7 us (14%)
  blocking collectives  63.4 us (10%)
  matrix products  50.6 us (8%)
  starting transfers between devices  35.2 us (6%)
  between operations  14.5 us (2%)
    psum x1, waiting for transfers between devices, on_device(): squares = lax.psum(jnp.sum(flat_in * flat_in, axis=1), 'ch')  75.1 us
    all_to_all x1, waiting for transfers between devices, on_device(): lax.all_to_all(section_one, 'ctx', split_axis=1, concat_axis=0, tiled=True)  48.9 us
    psum x1, waiting for transfers between devices, on_device(): one_total, two_total = lax.psum((one_part, two_part), ('ctx', 'ch'))  39.4 us
    reduce_sum x1, other arithmetic, on_device(): gain_part = jnp.sum(grad_normed * hat, axis=0)  31.9 us
    psum x1, blocking collectives, on_device(): lax.psum(jnp.sum(scaled * hat, axis=1).astype(jnp.bfloat16), 'ch')  31.7 us
    psum x1, blocking collectives, on_device(): gain_total, taps_total = lax.psum((gain_part, tap_part), 'ctx')  31.7 us
    all_to_all x1, waiting for transfers between devices, on_device(): lax.all_to_all(section_two, 'ctx', split_axis=0, concat_axis=1, tiled=True)  31.2 us
    unnamed x33, local copies, waits for them, and re-layouts  30.4 us
  transfers between devices with their start and end apart: 9, of which 9 were waited for; matrix products, arithmetic and copies ran while one was open for 26% of the time, Pallas kernels for 0%

commit v1 on v0

--- a/solution.py
+++ b/solution.py
@@ -7,6 +7,10 @@
 OUTER = 512
 INNER = 512
 WIDTH = 1024
+
+
+def mix_stacks_all_on_mesh(slab_in, ax_name):
+    return jnp.sum(jax.lax.all_gather(slab_in, ax_name), axis=0)
 
 
 def shifted(value, axis, steps):
@@ -80,7 +84,9 @@
     gain_total, taps_total = lax.psum((gain_part, tap_part), "ctx")
     scaled = grad_normed * norm_gain
     row_mean = (
-        lax.psum(jnp.sum(scaled * hat, axis=1).astype(jnp.bfloat16), "ch").astype(jnp.float32)
+        mix_stacks_all_on_mesh(jnp.sum(scaled * hat, axis=1).astype(jnp.bfloat16), "ch").astype(
+            jnp.float32
+        )
         / WIDTH
     )
     input_grad = (

time: 606 us -> 606 us (level)
    psum x1 -> x0, blocking collectives: 31.7 us -> none  [on_device(): lax.psum(jnp.sum(scaled * hat, axis=1).astype(jnp.bfloat16), 'ch')]
    all_gather x0 -> x1, blocking collectives: none -> 28.5 us  [mix_stacks_all_on_mesh(): return jnp.sum(jax.lax.all_gather(slab_in, ax_name), axis=0)]
where the time goes in v1:
time: 606 us; the launch traced here: 596 us
  waiting for transfers between devices  243 us (40%)
  local copies, waits for them, and re-layouts  108 us (18%)
  other arithmetic  84.9 us (14%)
  blocking collectives  59.3 us (10%)
  matrix products  50.6 us (8%)
  starting transfers between devices  35.2 us (6%)
  between operations  14.5 us (2%)
    psum x1, waiting for transfers between devices, on_device(): squares = lax.psum(jnp.sum(flat_in * flat_in, axis=1), 'ch')  75.1 us
    all_to_all x1, waiting for transfers between devices, on_device(): lax.all_to_all(section_one, 'ctx', split_axis=1, concat_axis=0, tiled=True)  48.9 us
    psum x1, waiting for transfers between devices, on_device(): one_total, two_total = lax.psum((one_part, two_part), ('ctx', 'ch'))  43.2 us
    reduce_sum x1, other arithmetic, on_device(): gain_part = jnp.sum(grad_normed * hat, axis=0)  31.9 us
    all_to_all x1, waiting for transfers between devices, on_device(): lax.all_to_all(section_two, 'ctx', split_axis=0, concat_axis=1, tiled=True)  31.2 us
    psum x1, blocking collectives, on_device(): gain_total, taps_total = lax.psum((gain_part, tap_part), 'ctx')  30.8 us
    unnamed x33, local copies, waits for them, and re-layouts  30.4 us
    all_to_all x1, waiting for transfers between devices, on_device(): lax.all_to_all(grad_section, 'ctx', split_axis=0, concat_axis=1, tiled=True)  29.1 us
  transfers between devices with their start and end apart: 9, of which 9 were waited for; matrix products, arithmetic and copies ran while one was open for 26% of the time, Pallas kernels for 0%

profile of v1, /device:TPU:1, one launch (start us, length us, event | category | flops | bytes accessed | tf_op | source)
XLA Modules:
  0.0 595.7 jit_solution(10027244180009093508)
XLA Ops:
  17.5 7.1 %copy.67 = f32[32,512,128]{2,1,0:T(8,128)} copy(bf16[32,512,128]{1,2,0:T(8,128)(2,1)} %copy.66) | data formatting | bytes 12582912 | tf_op jit(solution)/shard_map/convert_element_type | solution.py:26
  24.6 75.1 %all-reduce.5.cloned.1.call-done = f32[16384]{0:T(1024)} async-done(((f32[16384]{0:T(1024)}), f32[16384]{0:T(1024)}) %all-reduce.5.cloned.1.call-update) | async-done | bytes 65552 | tf_op jit(solution)/shard_map/psum | solution.py:27
  106.2 9.4 %collective-permute-start = (bf16[2,128]{1,0:T(2,128)(2,1)S(1)}, bf16[2,128]{1,0:T(2,128)(2,1)S(1)}, u32[]{:S(2)}, u32[]{:S(2)}) collective-permute-start(bf16[2,128]{1,0:T(2,128)(2,1)S(1)} %slice.68), channel_id=1, source_target_pairs={{0,8},{8,16},{16,24},{24,32},{32,40},{40,48},{48,56},{56,64},{64,7... | collective-permute-start | bytes 1544 | tf_op jit(solution)/shard_map/ppermute | solution.py:19
  132.2 7.9 %copy.78 = bf16[32,512,128]{2,0,1:T(8,128)(2,1)} copy(bf16[32,512,128]{1,2,0:T(8,128)(2,1)} %convert_bitcast_fusion.3) | data formatting | bytes 8388608 | tf_op jit(solution)/shard_map/convert_element_type | solution.py:44
  152.6 48.9 %all-to-all-done.2 = bf16[32,512,128]{2,0,1:T(8,128)(2,1)} async-done(((bf16[32,512,128]{2,0,1:T(8,128)(2,1)}), bf16[32,512,128]{2,0,1:T(8,128)(2,1)}, u32[]{:S(2)}, u32[]{:S(2)}) %all-to-all-start.2) | async-done | bytes 4194336 | tf_op jit(solution)/shard_map/all_to_all | solution.py:46
  207.0 7.6 %copy.72 = bf16[512,32,128]{0,2,1:T(8,128)(2,1)} copy(bf16[512,32,128]{2,1,0:T(8,128)(2,1)} %param.12) | data formatting | bytes 8388608 | tf_op args[5]
  223.8 9.9 %copy.81 = f32[512,32,128]{0,2,1:T(8,128)} copy(f32[512,32,128]{2,1,0:T(8,128)} %bitcast.102) | data formatting | bytes 16777216 | tf_op jit(solution)/shard_map/convert_element_type | solution.py:48
  233.7 8.9 %convert_bitcast_fusion.2 = bf16[512,32,128]{0,2,1:T(8,128)(2,1)} fusion(bf16[512,512]{1,0:T(8,128)(2,1)S(1)} %copy-done, f32[512,32,128]{0,2,1:T(8,128)} %copy.81, bf16[512,32,128]{0,2,1:T(8,128)(2,1)} %copy.72), kind=kOutput, calls=%fused_computation.66 | convolution fusion | flops 2155872256 | bytes 17301504 | tf_op jit(solution)/shard_map/ijc,ik->kjc/dot_general | solution.py:49
  242.6 7.9 %copy.82 = bf16[512,32,128]{2,1,0:T(8,128)(2,1)} copy(bf16[512,32,128]{0,2,1:T(8,128)(2,1)} %convert_bitcast_fusion.2) | data formatting | bytes 8388608 | tf_op jit(solution)/shard_map/convert_element_type | solution.py:51
  250.6 11.9 %all-to-all-done = bf16[32,512,128]{2,0,1:T(8,128)(2,1)} async-done(((bf16[32,512,128]{2,0,1:T(8,128)(2,1)}), bf16[32,512,128]{2,0,1:T(8,128)(2,1)}, u32[]{:S(2)}, u32[]{:S(2)}) %all-to-all-start) | async-done | bytes 4194336 | tf_op jit(solution)/shard_map/all_to_all | solution.py:53
  271.7 12.6 %fusion.29 = (bf16[512,32,128]{0,2,1:T(8,128)(2,1)}, bf16[512,32,128]{0,2,1:T(8,128)(2,1)}) fusion(f32[512,32,128]{0,2,1:T(8,128)} %copy.81, bf16[512,32,128]{0,2,1:T(8,128)(2,1)S(1)} %copy-done.2, bf16[512,512]{1,0:T(8,128)(2,1)S(1)} %copy-done, bf16[512,32,128]{2,1,0:T(8,128)(2,1)S(1)} %bitcast.100), kind=kOutput, calls=%fused_computation.53 | convolution fusion | flops 2157969408 | bytes 25690112 | tf_op jit(solution)/shard_map/kjc,ik->ijc/dot_general | solution.py:54
  284.4 7.9 %copy.73 = bf16[512,32,128]{2,1,0:T(8,128)(2,1)} copy(bf16[512,32,128]{0,2,1:T(8,128)(2,1)} %get-tuple-element.48) | data formatting | bytes 8388608 | tf_op jit(solution)/shard_map/convert_element_type | solution.py:58
  292.3 31.2 %all-to-all-done.3 = bf16[512,32,128]{2,1,0:T(8,128)(2,1)} async-done(((bf16[512,32,128]{2,1,0:T(8,128)(2,1)}), bf16[512,32,128]{2,1,0:T(8,128)(2,1)}, u32[]{:S(2)}, u32[]{:S(2)}) %all-to-all-start.3) | async-done | bytes 4194336 | tf_op jit(solution)/shard_map/all_to_all | solution.py:52
  328.5 7.8 %copy.87 = bf16[512,32,128]{2,1,0:T(8,128)(2,1)} copy(bf16[512,32,128]{0,2,1:T(8,128)(2,1)} %get-tuple-element.47) | data formatting | bytes 8388608
  336.4 11.0 %fusion.35 = f32[512,512]{1,0:T(8,128)} fusion(bf16[512,32,128]{2,1,0:T(8,128)(2,1)} %bitcast.101, f32[512,32,128]{0,2,1:T(8,128)} %copy.81, bf16[512,32,128]{0,2,1:T(8,128)(2,1)} %copy.72), kind=kOutput, calls=%fused_computation.73 | convolution fusion | flops 2153775104 | bytes 17825792 | tf_op jit(solution)/shard_map/ijc,kjc->ik/dot_general | solution.py:59
  355.1 29.1 %all-to-all-done.1 = bf16[512,32,128]{2,1,0:T(8,128)(2,1)} async-done(((bf16[512,32,128]{2,1,0:T(8,128)(2,1)}), bf16[512,32,128]{2,1,0:T(8,128)(2,1)}, u32[]{:S(2)}, u32[]{:S(2)}) %all-to-all-start.1) | async-done | bytes 4194336 | tf_op jit(solution)/shard_map/all_to_all | solution.py:60
  393.1 10.3 %multiply_reduce_fusion = (f32[128]{0:T(128)S(1)}, f32[32,512,128]{1,2,0:T(8,128)}) fusion(f32[128]{0:T(128)S(1)} %copy-done.12, f32[32,512]{1,0:T(8,128)S(1)} %mul.250, bf16[32,512,128]{1,2,0:T(8,128)(2,1)} %copy.66, bf16[32,512,128]{2,1,0:T(8,128)(2,1)} %bitcast.108, bf16[512,512]{1,0:T(8,128)(2,1)S(1)} %copy-done.11), kind=kOutput, calls=%fused_computation.55 | convolution fusion | flops 2162163712 | bytes 17368064 | tf_op jit(solution)/shard_map/ikc,jk->ijc/dot_general | solution.py:63
  403.4 8.9 %copy.76 = f32[32,512,128]{2,1,0:T(8,128)} copy(f32[32,512,128]{1,2,0:T(8,128)} %get-tuple-element.56) | data formatting | bytes 16777216 | tf_op jit(solution)/shard_map/ikc,jk->ijc/transpose | solution.py:63
  413.0 14.0 %fusion.22 = (f32[128]{0:T(128)S(1)}, f32[128]{0:T(128)S(1)}, f32[128]{0:T(128)S(1)}, f32[128]{0:T(128)S(1)}, f32[128]{0:T(128)S(1)}, /*index=5*/f32[16384,128]{1,0:T(8,128)S(1)}) fusion(bf16[16384,128]{1,0:T(8,128)(2,1)} %copy-done.3, bf16[2,128]{1,0:T(2,128)(2,1)S(1)} %collective-permute-done, bf16[16384,128]{1,0:T(8,128)(2,1)} %copy-done.5, ...), kind=kLoop, calls=%fused_computation.41 | loop fusion | flops 60816768 | bytes 37753344 | tf_op jit(solution)/shard_map/reduce_sum | solution.py:81
  438.1 31.9 %multiply_reduce_fusion.1 = (f32[128]{0:T(128)S(1)}, bf16[16384]{0:T(1024)(128)(2,1)S(1)}, f32[16384,128]{1,0:T(8,128)}) fusion(f32[32,512,128]{2,1,0:T(8,128)} %copy.67, f32[16384]{0:T(1024)S(1)} %add_rsqrt_fusion, f32[128]{0:T(128)S(1)} %copy-done.12, f32[2,128]{1,0:T(2,128)S(1)} %collective-permute-done.2, f32[16384,128]{1,0:T(8,128)} %copy-done.6, ...), kind=kLoop, calls=%fused_computation.57 | loop fusion | flops 44023680 | bytes 33658880 | tf_op jit(solution)/shard_map/reduce_sum | solution.py:83
  470.1 28.5 %all-gather = bf16[131072]{0:T(1024)(128)(2,1)S(1)} all-gather(bf16[16384]{0:T(1024)(128)(2,1)S(1)} %get-tuple-element.31), channel_id=2, replica_groups=mesh['ctx'=16,'ch'=8] {'ch'}, dimensions={0}, use_global_device_ids=true | all-gather | bytes 294912 | tf_op jit(solution)/shard_map/all_gather | solution.py:13
  498.9 11.5 %multiply_convert_fusion.1 = bf16[16384,128]{1,0:T(8,128)(2,1)} fusion(f32[16384,128]{1,0:T(8,128)} %get-tuple-element.44, f32[32,512,128]{2,1,0:T(8,128)} %copy.67, f32[16384]{0:T(1024)S(1)} %convert_multiply_fusion.15, f32[128]{0:T(128)S(1)} %copy-done.12, f32[16384]{0:T(1024)S(1)} %add_rsqrt_fusion), kind=kLoop, calls=%fused_computation.58 | loop fusion | flops 12582912 | bytes 21103104 | tf_op jit(solution)/shard_map/convert_element_type | solution.py:94
  510.4 30.8 %all-reduce.1 = (f32[128]{0:T(128)S(1)}, f32[2,3,128]{2,1,0:T(4,128)S(1)}) all-reduce(f32[128]{0:T(128)S(1)} %get-tuple-element.30, f32[2,3,128]{2,1,0:T(4,128)S(1)} %pad_maximum_fusion.3), channel_id=1, replica_groups=mesh['ctx'=16,'ch'=8] {'ctx'}, use_global_device_ids=true, to_apply=%region_7.0 | all-reduce | flops 896 | bytes 7168 | tf_op jit(solution)/shard_map/psum | solution.py:84
  542.4 43.2 %all-reduce.7.cloned.1.call-done = (f32[512,512]{1,0:T(8,128)}, f32[512,512]{1,0:T(8,128)}) async-done(((f32[512,512]{1,0:T(8,128)}, f32[512,512]{1,0:T(8,128)}), (f32[512,512]{1,0:T(8,128)}, f32[512,512]{1,0:T(8,128)})) %all-reduce.7.cloned.1.call-update) | async-done | bytes 2097168 | tf_op jit(solution)/shard_map/psum | solution.py:67
  (72 shorter events, 107.7 us)
Async XLA Ops:
  7.2 226.5 %copy-start = (bf16[512,512]{1,0:T(8,128)(2,1)S(1)}, bf16[512,512]{1,0:T(8,128)(2,1)}, u32[]{:S(2)}) copy-start(bf16[512,512]{1,0:T(8,128)(2,1)} %param.11) | copy-start | bytes 1572868
  7.2 92.5 %all-reduce.5.cloned.1.call-start = ((), (), s32[]{:S(2)}) async-start(), calls=%async_computation.4 | async-start | bytes 131072 | tf_op jit(solution)/shard_map/psum | solution.py:27
  13.7 87.0 %copy-start.12 = (f32[128]{0:T(128)S(1)}, f32[128]{0:T(128)}, u32[]{:S(2)}) copy-start(f32[128]{0:T(128)} %param.8) | copy-start | bytes 1540
  24.6 91.1 %copy-start.13 = (f32[2,3,128]{2,0,1:T(2,128)S(1)}, f32[2,3,128]{2,0,1:T(2,128)}, u32[]{:S(2)}) copy-start(f32[2,3,128]{2,0,1:T(2,128)} %param.9) | copy-start | bytes 9220
  99.7 16.6 %copy-start.9 = (bf16[32,512,128]{2,1,0:T(8,128)(2,1)S(1)}, bf16[32,512,128]{2,1,0:T(8,128)(2,1)}, u32[]{:S(2)}) copy-start(bf16[32,512,128]{2,1,0:T(8,128)(2,1)} %param.13) | copy-start | bytes 12582916
  106.2 16.6 %copy-start.3 = (bf16[16384,128]{1,0:T(8,128)(2,1)}, bf16[16384,128]{1,0:T(8,128)(2,1)S(1)}, u32[]{:S(2)}) copy-start(bf16[16384,128]{1,0:T(8,128)(2,1)S(1)} %multiply_convert_fusion.2) | copy-start | bytes 12582916
  106.2 10.1 %collective-permute-start = (bf16[2,128]{1,0:T(2,128)(2,1)S(1)}, bf16[2,128]{1,0:T(2,128)(2,1)S(1)}, u32[]{:S(2)}, u32[]{:S(2)}) collective-permute-start(bf16[2,128]{1,0:T(2,128)(2,1)S(1)} %slice.68), channel_id=1, source_target_pairs={{0,8},{8,16},{16,24},{24,32},{32,40},{40,48},{48,56},{56,64},{64,7... | collective-permute-start | bytes 1544 | tf_op jit(solution)/shard_map/ppermute | solution.py:19
  122.8 3.0 copy-start.5
  122.8 5.0 copy-start.11
  125.9 1.9 copy-start.7
  140.1 61.4 %all-to-all-start.2 = ((bf16[32,512,128]{2,0,1:T(8,128)(2,1)}), bf16[32,512,128]{2,0,1:T(8,128)(2,1)}, u32[]{:S(2)}, u32[]{:S(2)}) async-start(bf16[32,512,128]{2,0,1:T(8,128)(2,1)} %copy.78), calls=%async_computation.2 | async-start | bytes 8388608 | tf_op jit(solution)/shard_map/all_to_all | solution.py:46
  201.5 61.0 %all-to-all-start = ((bf16[32,512,128]{2,0,1:T(8,128)(2,1)}), bf16[32,512,128]{2,0,1:T(8,128)(2,1)}, u32[]{:S(2)}, u32[]{:S(2)}) async-start(bf16[32,512,128]{2,0,1:T(8,128)(2,1)} %copy.68), calls=%async_computation | async-start | bytes 8388608 | tf_op jit(solution)/shard_map/all_to_all | solution.py:53
  262.5 61.0 %all-to-all-start.3 = ((bf16[512,32,128]{2,1,0:T(8,128)(2,1)}), bf16[512,32,128]{2,1,0:T(8,128)(2,1)}, u32[]{:S(2)}, u32[]{:S(2)}) async-start(bf16[512,32,128]{2,1,0:T(8,128)(2,1)} %copy.82), calls=%async_computation.3 | async-start | bytes 8388608 | tf_op jit(solution)/shard_map/all_to_all | solution.py:52
  267.6 4.1 copy-start.2
  271.7 12.6 %copy-start.4 = (bf16[16,32,32,128]{3,2,1,0:T(8,128)(2,1)}, bf16[16,32,32,128]{3,2,1,0:T(8,128)(2,1)S(1)}, u32[]{:S(2)}) copy-start(bf16[16,32,32,128]{3,2,1,0:T(8,128)(2,1)S(1)} %copy.70) | copy-start | bytes 12582916
  323.4 60.7 %all-to-all-start.1 = ((bf16[512,32,128]{2,1,0:T(8,128)(2,1)}), bf16[512,32,128]{2,1,0:T(8,128)(2,1)}, u32[]{:S(2)}, u32[]{:S(2)}) async-start(bf16[512,32,128]{2,1,0:T(8,128)(2,1)} %copy.73), calls=%async_computation.1 | async-start | bytes 8388608 | tf_op jit(solution)/shard_map/all_to_all | solution.py:60
  328.5 257.0 %all-reduce.7.cloned.1.call-start = ((), (), s32[]{:S(2)}) async-start(), calls=%async_computation.5 | async-start | bytes 4194304 | tf_op jit(solution)/shard_map/psum | solution.py:67
  384.2 5.5 copy-start.8
  387.8 1.9 copy-start.10
  427.0 3.3 copy-start.6
  430.3 5.9 collective-permute-start.2
  432.9 5.3 collective-permute-start.1
  498.9 89.7 %copy-start.1 = (bf16[512,512]{1,0:T(8,128)(2,1)S(1)}, bf16[512,512]{1,0:T(8,128)(2,1)}, u32[]{:S(2)}) copy-start(bf16[512,512]{1,0:T(8,128)(2,1)} %param.11) | copy-start | bytes 1572868
Sparse Core Ops, SparseCore 0:
  17.6 82.0 all-reduce.4
  435.0 150.5 all-reduce.6
